TPU v7x, 512 devices: a whole 4x8x8 slice. The times are simulated.
512 devices in a mesh: segment: 16 (over z, core), mp: 32 (over y, x).
Axes of the slice: x: 4, y: 8, z: 8, core: 2. Of those that a mesh axis runs over, the one named last changes fastest.
Arguments:
- rows: bfloat16 [16, 2, 128, 8192], P('segment', None, None, 'mp'), may hold values from -6 to 6
- carry: bfloat16 [16, 128, 8192], P('segment', None, 'mp'), may hold values from -6 to 6
- weights: bfloat16 [16, 2, 8192, 4096], P('segment', None, None, 'mp'), may hold values from -1.1932427 to 1.1932427
- neighbours: int32 [16, 2, 2, 2], P('segment'), may hold values from 0 to 7, all different within a row
Outputs:
- passed: bfloat16 [16, 128, 8192], P('segment', None, 'mp')
- returned: bfloat16 [16, 128, 8192], P('segment', None, 'mp')
- kv_grad: bfloat16 [1024, 2, 4096], P(None, None, 'mp')
Inputs may be any that keep to these rules, and one draw needn't show every extreme that they name: Each group's 2 neighbours are different pool blocks; pool blocks are numbered by encoder segment in order, then by row.
All inputs are finite; a program needn't handle non-finite values.
Results may differ from a plain program's by a relative error of at most 0.02.
The roundings to bfloat16 on the way count: a program that leaves them out, or rounds other values in their place, can miss the bound.
Values may be sent and summed in bfloat16 or wider, within the bound.
No kernel may reach another device: no remote copies, remote signals or barrier semaphores. Data moves between devices by JAX's collectives and lax.ppermute only.
A program may use at most 64 MiB of HBM per device.

v0:
```python
import math
import jax
import jax.numpy as jnp
from jax import lax
from jax.sharding import PartitionSpec as P

GROUP = 64
NBLEN = 128
NEIGH = 2


def from_behind(x, axis, by):
    devices = lax.axis_size(axis)
    return lax.ppermute(x, axis, [(i, (i + by) % devices) for i in range(devices)])


def attend(queries, key_rows, score_scale):
    scores = (
        jnp.einsum("cqd,ckd->cqk", queries, key_rows, preferred_element_type=jnp.float32)
        * score_scale
    )
    soft = jax.nn.softmax(scores, axis=-1)
    return (soft, soft.astype(jnp.bfloat16))


def attend_back(queries, key_rows, value_rows, soft, rounded, upstream, score_scale):
    d_soft = jnp.einsum("cqd,ckd->cqk", upstream, value_rows, preferred_element_type=jnp.float32)
    grad_values = jnp.einsum("cqk,cqd->ckd", rounded, upstream, preferred_element_type=jnp.float32)
    d_scores = soft * (d_soft - jnp.sum(d_soft * soft, axis=-1, keepdims=True))
    grad_queries = (
        jnp.einsum("cqk,ckd->cqd", d_scores, key_rows.astype(jnp.float32)) * score_scale
    ).astype(jnp.bfloat16)
    grad_keys = jnp.einsum("cqk,cqd->ckd", d_scores, queries.astype(jnp.float32)) * score_scale
    return (grad_queries, grad_keys, grad_values)


def per_device(rows, carry, weights, neighbours):
    segments = lax.axis_size("segment")
    encoders = segments // 4
    first_encoder = segments - encoders
    is_encoder = lax.axis_index("segment") >= first_encoder
    local_rows = rows[0]
    local_carry = carry[0]
    full_rows, full_carry = (
        lax.all_gather(local_rows, "mp", axis=2, tiled=True),
        lax.all_gather(local_carry, "mp", axis=1, tiled=True),
    )
    tokens = local_rows.shape[1]
    width = full_rows.shape[2]
    head = weights.shape[3]
    w_query = weights[0, 0]
    w_out = weights[0, 1]

    def encode():
        flat = full_rows.reshape(2 * tokens, width)
        keyval = jnp.concatenate(
            [
                jnp.dot(flat, w_query, preferred_element_type=jnp.float32),
                jnp.dot(flat, w_out, preferred_element_type=jnp.float32),
            ],
            axis=-1,
        ).astype(jnp.bfloat16)
        return (keyval, jnp.zeros((2 * tokens, head), jnp.bfloat16))

    def decode():
        queries = jnp.dot(
            full_rows.reshape(2 * tokens, width), w_query, preferred_element_type=jnp.float32
        ).astype(jnp.bfloat16)
        return (jnp.zeros((2 * tokens, 2 * head), jnp.bfloat16), queries)

    encoded, queries = lax.cond(is_encoder, encode, decode)
    per_encoder = 2 * tokens // NBLEN
    pool_blocks = encoders * per_encoder
    collected = lax.all_gather(encoded, "segment", axis=0, tiled=True)
    pool = collected[first_encoder * 2 * tokens :].reshape(pool_blocks, NBLEN, 2 * head)
    groups = tokens // GROUP
    local_nbr = neighbours[0]
    score_scale = 1.0 / math.sqrt(head)
    query_blocks = queries.reshape(2, groups, GROUP, head)

    def fetch(batch):
        picked = pool[local_nbr[batch]].reshape(groups, NEIGH * NBLEN, 2 * head)
        return (picked[..., :head], picked[..., head:])

    keys_fwd, values_fwd = fetch(0)
    soft_fwd, rounded_fwd = attend(query_blocks[0], keys_fwd, score_scale)
    mixed = jnp.einsum(
        "cqk,ckd->cqd", rounded_fwd, values_fwd, preferred_element_type=jnp.float32
    ).astype(jnp.bfloat16)
    mixed_flat = mixed.reshape(tokens, head)
    piece = w_out
    out_sum = (
        lax.psum_scatter(
            lax.dot_general(
                piece, mixed_flat, (((1,), (1,)), ((), ())), preferred_element_type=jnp.float32
            ).astype(jnp.bfloat16),
            "mp",
            scatter_dimension=0,
            tiled=True,
        )
        .astype(jnp.float32)
        .T
    )
    forward_rows = (local_rows[0].astype(jnp.float32) + out_sum).astype(jnp.bfloat16)
    forward_rows = jnp.where(is_encoder, local_carry, forward_rows)
    passed = from_behind(forward_rows[None], "segment", 1)
    upstream = (
        jnp.dot(full_carry, w_out, preferred_element_type=jnp.float32)
        .astype(jnp.bfloat16)
        .reshape(groups, GROUP, head)
    )
    keys_back, values_back = fetch(1)
    soft_back, rounded_back = attend(query_blocks[1], keys_back, score_scale)
    grad_queries, grad_keys, grad_values = attend_back(
        query_blocks[1], keys_back, values_back, soft_back, rounded_back, upstream, score_scale
    )
    grad_flat = grad_queries.reshape(tokens, head)
    piece = w_query
    grad_input = (
        lax.psum_scatter(
            lax.dot_general(
                piece, grad_flat, (((1,), (1,)), ((), ())), preferred_element_type=jnp.float32
            ).astype(jnp.bfloat16),
            "mp",
            scatter_dimension=0,
            tiled=True,
        )
        .astype(jnp.float32)
        .T
    )
    back = local_carry.astype(jnp.float32) + grad_input
    back_rows = jnp.where(is_encoder, local_carry, back.astype(jnp.bfloat16))
    returned = from_behind(back_rows[None], "segment", -1)
    onehot = (
        local_nbr[1][..., None] == jnp.arange(pool_blocks, dtype=jnp.int32)[None, None, :]
    ).astype(jnp.float32)
    grad_keyval = jnp.concatenate([grad_keys, grad_values], axis=-1).reshape(
        groups, NEIGH, NBLEN, 2 * head
    )
    contrib = jnp.einsum("cbp,cbrf->prf", onehot, grad_keyval)
    contrib = jnp.where(is_encoder, jnp.zeros_like(contrib), contrib)
    pooled = lax.psum(contrib.astype(jnp.bfloat16), "segment").astype(jnp.float32)
    kv_grad = pooled.reshape(pool_blocks * NBLEN, 2, head).astype(jnp.bfloat16)
    return (passed, returned, kv_grad)


def solution(mesh):
    placed = (
        P("segment", None, None, "mp"),
        P("segment", None, "mp"),
        P("segment", None, None, "mp"),
        P("segment", None, None, None),
    )
    return jax.shard_map(
        per_device,
        mesh=mesh,
        in_specs=placed,
        out_specs=(P("segment", None, "mp"), P("segment", None, "mp"), P(None, None, "mp")),
        check_vma=False,
    )
```

profile of v0, /device:TPU:1, one launch (start us, length us, event | category | flops | bytes accessed | tf_op | source)
XLA Modules:
  0.0 812.3 jit_solution(813906581693303927)
XLA Ops:
  7.2 0.0 all-gather.8.cloned.1.call-start
  7.2 0.7 all-gather.8.cloned.1.call-update
  7.9 0.0 all-gather.10.cloned.1.call-start
  7.9 0.7 all-gather.10.cloned.1.call-update
  8.6 0.0 all-gather.6.cloned.1.call-start
  8.7 3.8 slice_bitcast_fusion
  12.5 89.2 %all-gather.8.cloned.1.call-done = bf16[1,2,128,8192]{3,2,1,0:T(8,128)(2,1)} async-done(((bf16[1,2,128,256]{3,2,1,0:T(8,128)(2,1)}), bf16[1,2,128,8192]{3,2,1,0:T(8,128)(2,1)}) %all-gather.8.cloned.1.call-update) | async-done | bytes 4194320 | tf_op jit(solution)/shard_map/all_gather | solution.py:45
  101.8 0.0 copy-start.4
  101.8 3.5 conditional.1
  101.8 3.4 convolution_convert_fusion
  105.3 0.0 copy-start.1
  105.3 0.6 copy-done.1
  105.9 0.0 all-gather.6.cloned.1.call-update
  106.0 0.0 reduce-scatter.5.cloned.1.call-start
  106.0 0.0 copy-done.4
  106.0 0.1 reshape.131
  106.1 79.5 %all-gather.10.cloned.1.call-done = bf16[1,128,8192]{2,1,0:T(8,128)(2,1)} async-done(((bf16[1,128,256]{2,1,0:T(8,128)(2,1)}), bf16[1,128,8192]{2,1,0:T(8,128)(2,1)}) %all-gather.10.cloned.1.call-update) | async-done | bytes 2097168 | tf_op jit(solution)/shard_map/all_gather | solution.py:46
  185.7 2.9 fusion.13
  188.6 45.9 %all-gather.6.cloned.1.call-done = bf16[4096,256]{1,0:T(8,128)(2,1)} async-done(((bf16[256,256]{1,0:T(8,128)(2,1)}), bf16[4096,256]{1,0:T(8,128)(2,1)}) %all-gather.6.cloned.1.call-update) | async-done | bytes 2097168 | tf_op jit(solution)/shard_map/all_gather | solution.py:74
  234.5 1.1 slice.67
  235.6 0.6 gather_fusion.1
  236.2 0.2 convolution_multiply_fusion.1
  236.3 0.4 fusion.37
  236.7 0.3 multiply_reduce_fusion
  236.9 0.3 fusion.12
  237.3 3.7 fusion.3
  241.0 0.0 reduce-scatter.5.cloned.1.call-update
  241.0 0.0 reduce-scatter.3.cloned.1.call-start
  241.0 0.1 reshape.123
  241.1 0.6 gather_fusion
  241.7 0.2 convolution_multiply_fusion.2
  241.9 0.2 fusion.38
  242.0 0.3 convolution_convert_fusion.5
  242.4 3.6 fusion.2
  246.0 0.0 reduce-scatter.3.cloned.1.call-update
  246.0 0.0 all-reduce.2.cloned.1.call-start
  246.1 0.1 copy.11
  246.1 0.3 fusion.28
  246.5 0.4 convolution_multiply_fusion
  246.9 0.1 reshape.119
  247.0 0.5 copy.12
  247.5 0.0 copy-start.2
  247.5 0.0 copy-start.3
  247.5 0.5 fusion.7
  248.0 0.6 copy.13
  248.6 1.0 convert_element_type.80
  249.6 0.0 all-reduce.2.cloned.1.call-update
  249.6 205.3 %reduce-scatter.5.cloned.1.call-done = bf16[256,128]{0,1:T(8,128)(2,1)} async-done(((bf16[8192,128]{0,1:T(8,128)(2,1)}), bf16[256,128]{0,1:T(8,128)(2,1)}) %reduce-scatter.5.cloned.1.call-update) | async-done | bytes 65552 | tf_op jit(solution)/shard_map/reduce_scatter | solution.py:120
  454.9 224.9 %reduce-scatter.3.cloned.1.call-done = bf16[256,128]{0,1:T(8,128)(2,1)} async-done(((bf16[8192,128]{0,1:T(8,128)(2,1)}), bf16[256,128]{0,1:T(8,128)(2,1)}) %reduce-scatter.3.cloned.1.call-update) | async-done | bytes 65552 | tf_op jit(solution)/shard_map/reduce_scatter | solution.py:93
  679.8 0.0 copy-done.2
  679.8 0.0 copy-done.3
  679.8 0.9 fusion.25
  680.7 6.9 collective-permute-start
  687.6 0.0 collective-permute-start.1
  687.6 114.5 %all-reduce.2.cloned.1.call-done = bf16[1024,2,128]{0,2,1:T(8,128)(2,1)} async-done(((bf16[1024,2,128]{0,2,1:T(8,128)(2,1)}), bf16[1024,2,128]{0,2,1:T(8,128)(2,1)}) %all-reduce.2.cloned.1.call-update) | async-done | bytes 524304 | tf_op jit(solution)/shard_map/psum | solution.py:142
  802.1 2.0 copy.14
  804.1 0.0 collective-permute-done
  804.1 0.0 collective-permute-done.1
  804.1 0.6 copy.25
  804.8 0.6 copy.26
  (7 shorter events, 0.1 us)
Async XLA Ops:
  7.2 94.6 %all-gather.8.cloned.1.call-start = ((), (), s32[]{:S(2)}) async-start(), calls=%async_computation.6 | async-start | bytes 4325376 | tf_op jit(solution)/shard_map/all_gather | solution.py:45
  7.9 177.8 %all-gather.10.cloned.1.call-start = ((), (), s32[]{:S(2)}) async-start(), calls=%async_computation.7 | async-start | bytes 2162688 | tf_op jit(solution)/shard_map/all_gather | solution.py:46
  8.6 225.9 %all-gather.6.cloned.1.call-start = ((), (), s32[]{:S(2)}) async-start(), calls=%async_computation.2 | async-start | bytes 2228224 | tf_op jit(solution)/shard_map/all_gather | solution.py:74
  101.8 4.2 copy-start.4
  105.3 0.7 copy-start.1
  106.0 348.9 %reduce-scatter.5.cloned.1.call-start = ((), (), s32[]{:S(2)}) async-start(), calls=%async_computation.4 | async-start | bytes 2162688 | tf_op jit(solution)/shard_map/reduce_scatter | solution.py:120
  241.0 438.8 %reduce-scatter.3.cloned.1.call-start = ((), (), s32[]{:S(2)}) async-start(), calls=%async_computation.3 | async-start | bytes 2162688 | tf_op jit(solution)/shard_map/reduce_scatter | solution.py:93
  246.0 556.2 %all-reduce.2.cloned.1.call-start = ((), (), s32[]{:S(2)}) async-start(), calls=%async_computation.5 | async-start | bytes 1048576 | tf_op jit(solution)/shard_map/psum | solution.py:142
  247.5 432.3 %copy-start.2 = (bf16[1,2,128,256]{3,2,1,0:T(8,128)(2,1)S(1)}, bf16[1,2,128,256]{3,2,1,0:T(8,128)(2,1)}, u32[]{:S(2)}) copy-start(bf16[1,2,128,256]{3,2,1,0:T(8,128)(2,1)} %param.6) | copy-start | bytes 393220
  247.5 432.3 %copy-start.3 = (bf16[1,128,256]{2,1,0:T(8,128)(2,1)S(1)}, bf16[1,128,256]{2,1,0:T(8,128)(2,1)}, u32[]{:S(2)}) copy-start(bf16[1,128,256]{2,1,0:T(8,128)(2,1)} %param.7) | copy-start | bytes 196612
  680.7 123.5 %collective-permute-start = (bf16[1,128,256]{2,1,0:T(8,128)(2,1)S(1)}, bf16[1,128,256]{2,1,0:T(8,128)(2,1)S(1)}, u32[]{:S(2)}, u32[]{:S(2)}) collective-permute-start(bf16[1,128,256]{2,1,0:T(8,128)(2,1)S(1)} %get-tuple-element.53), channel_id=1, source_target_pairs={{0,32},{32,64},{64,96},{96,128},{128,160},{160,192},{192,224},{224... | collective-permute-start | bytes 196616 | tf_op jit(solution)/shard_map/ppermute | solution.py:14
  687.6 116.5 %collective-permute-start.1 = (bf16[1,128,256]{2,1,0:T(8,128)(2,1)S(1)}, bf16[1,128,256]{2,1,0:T(8,128)(2,1)S(1)}, u32[]{:S(2)}, u32[]{:S(2)}) collective-permute-start(bf16[1,128,256]{2,1,0:T(8,128)(2,1)S(1)} %get-tuple-element.52), channel_id=1, source_target_pairs={{0,480},{32,0},{64,32},{96,64},{128,96},{160,128},{192,160},{224,1... | collective-permute-start | bytes 196616 | tf_op jit(solution)/shard_map/ppermute | solution.py:14
Sparse Core Ops, SparseCore 0:
  11.0 90.6 all-gather.7
  104.8 80.7 all-gather.9
  188.4 46.0 all-gather.5
  241.1 213.7 reduce-scatter.4
  459.8 219.9 reduce-scatter.2
  682.5 119.5 all-reduce.1
where the time goes:
time: 813 us; the launch traced here: 812 us
  waiting for transfers between devices  761 us (94%)
  matrix products  16.1 us (2%)
  between operations  14.3 us (2%)
  local copies, waits for them, and re-layouts  12.4 us (2%)
    reduce_scatter x1, waiting for transfers between devices, per_device(): lax.psum_scatter(lax.dot_general(piece, mixed_flat, (((1,), (1,)), ((), (...  225 us
    reduce_scatter x1, waiting for transfers between devices, per_device(): lax.psum_scatter(lax.dot_general(piece, grad_flat, (((1,), (1,)), ((), ()...  205 us
    psum x1, waiting for transfers between devices, per_device(): lax.psum(contrib.astype(jnp.bfloat16), 'segment').astype(jnp.float32)  115 us
    all_gather x1, waiting for transfers between devices, per_device(): lax.all_gather(local_rows, 'mp', axis=2, tiled=True)  89.2 us
    all_gather x1, waiting for transfers between devices, per_device(): lax.all_gather(local_carry, 'mp', axis=1, tiled=True)  79.5 us
    all_gather x1, waiting for transfers between devices, per_device(): collected = lax.all_gather(encoded, 'segment', axis=0, tiled=True)  45.9 us
  transfers between devices with their start and end apart: 8, of which 6 were waited for; matrix products, arithmetic and copies ran while one was open for 3% of the time, Pallas kernels for 0%

commit v1 on v0

--- a/solution.py
+++ b/solution.py
@@ -139,7 +139,9 @@
     )
     contrib = jnp.einsum("cbp,cbrf->prf", onehot, grad_keyval)
     contrib = jnp.where(is_encoder, jnp.zeros_like(contrib), contrib)
-    pooled = lax.psum(contrib.astype(jnp.bfloat16), "segment").astype(jnp.float32)
+    pooled = jnp.sum(lax.all_gather(contrib.astype(jnp.bfloat16), "segment"), axis=0).astype(
+        jnp.float32
+    )
     kv_grad = pooled.reshape(pool_blocks * NBLEN, 2, head).astype(jnp.bfloat16)
     return (passed, returned, kv_grad)
 

time: 813 us -> 771 us (0.948)
  waiting for transfers between devices: 761 us -> 715 us
    psum x1 -> x0, waiting for transfers between devices: 115 us -> none  [per_device(): lax.psum(contrib.astype(jnp.bfloat16), 'segment').astype(jnp.float32)]
    all_gather x0 -> x1, waiting for transfers between devices: none -> 66.1 us  [per_device(): lax.all_gather(contrib.astype(jnp.bfloat16), 'segment')]
  transfers between devices with their start and end apart: 8 -> 8, of which waited for: 6 -> 7; matrix products, arithmetic and copies ran while one was open for 3% -> 2% of each run, Pallas kernels for 0% -> 0%
where the time goes in v1:
time: 771 us
  waiting for transfers between devices  715 us (93%)
  matrix products  16.9 us (2%)
  between operations  14.3 us (2%)
  local copies, waits for them, and re-layouts  9.81 us (1%)
    reduce_scatter x1, waiting for transfers between devices, per_device(): lax.psum_scatter(lax.dot_general(piece, mixed_flat, (((1,), (1,)), ((), (...  225 us
    reduce_scatter x1, waiting for transfers between devices, per_device(): lax.psum_scatter(lax.dot_general(piece, grad_flat, (((1,), (1,)), ((), ()...  206 us
    all_gather x1, waiting for transfers between devices, per_device(): lax.all_gather(local_rows, 'mp', axis=2, tiled=True)  89.2 us
    all_gather x1, waiting for transfers between devices, per_device(): lax.all_gather(local_carry, 'mp', axis=1, tiled=True)  79.5 us
    all_gather x1, waiting for transfers between devices, per_device(): lax.all_gather(contrib.astype(jnp.bfloat16), 'segment')  66.1 us
    all_gather x1, waiting for transfers between devices, per_device(): collected = lax.all_gather(encoded, 'segment', axis=0, tiled=True)  45.9 us
  transfers between devices with their start and end apart: 8, of which 7 were waited for; matrix products, arithmetic and copies ran while one was open for 2% of the time, Pallas kernels for 0%

profile of v1, /device:TPU:1, one launch (start us, length us, event | category | flops | bytes accessed | tf_op | source)
XLA Modules:
  0.0 770.7 jit_solution(9426132704635546077)
XLA Ops:
  7.2 0.0 all-gather.10.cloned.1.call-start
  7.2 0.7 all-gather.10.cloned.1.call-update
  7.9 0.0 all-gather.12.cloned.1.call-start
  7.9 0.7 all-gather.12.cloned.1.call-update
  8.6 0.0 all-gather.8.cloned.1.call-start
  8.7 3.8 slice_bitcast_fusion
  12.5 89.2 %all-gather.10.cloned.1.call-done = bf16[1,2,128,8192]{3,2,1,0:T(8,128)(2,1)} async-done(((bf16[1,2,128,256]{3,2,1,0:T(8,128)(2,1)}), bf16[1,2,128,8192]{3,2,1,0:T(8,128)(2,1)}) %all-gather.10.cloned.1.call-update) | async-done | bytes 4194320 | tf_op jit(solution)/shard_map/all_gather | solution.py:45
  101.8 0.0 copy-start.4
  101.8 3.5 conditional.1
  101.8 3.4 convolution_convert_fusion
  105.3 0.0 copy-start.1
  105.3 0.6 copy-done.1
  105.9 0.0 all-gather.8.cloned.1.call-update
  106.0 0.0 reduce-scatter.5.cloned.1.call-start
  106.0 0.0 copy-done.4
  106.0 0.1 reshape.131
  106.1 79.5 %all-gather.12.cloned.1.call-done = bf16[1,128,8192]{2,1,0:T(8,128)(2,1)} async-done(((bf16[1,128,256]{2,1,0:T(8,128)(2,1)}), bf16[1,128,8192]{2,1,0:T(8,128)(2,1)}) %all-gather.12.cloned.1.call-update) | async-done | bytes 2097168 | tf_op jit(solution)/shard_map/all_gather | solution.py:46
  185.7 2.9 fusion.13
  188.6 45.9 %all-gather.8.cloned.1.call-done = bf16[4096,256]{1,0:T(8,128)(2,1)} async-done(((bf16[256,256]{1,0:T(8,128)(2,1)}), bf16[4096,256]{1,0:T(8,128)(2,1)}) %all-gather.8.cloned.1.call-update) | async-done | bytes 2097168 | tf_op jit(solution)/shard_map/all_gather | solution.py:74
  234.5 1.1 slice.67
  235.6 0.6 gather_fusion.1
  236.2 0.2 convolution_multiply_fusion.1
  236.3 0.4 fusion.37
  236.7 0.3 multiply_reduce_fusion
  236.9 0.3 fusion.12
  237.3 3.7 fusion.3
  241.0 0.0 reduce-scatter.5.cloned.1.call-update
  241.0 0.0 reduce-scatter.3.cloned.1.call-start
  241.1 0.1 reshape.123
  241.2 0.6 gather_fusion
  241.7 0.2 convolution_multiply_fusion.2
  241.9 0.2 fusion.38
  242.1 0.3 convolution_convert_fusion.5
  242.4 3.6 fusion.2
  246.0 0.0 reduce-scatter.3.cloned.1.call-update
  246.0 0.0 all-gather.14.cloned.1.call-start
  246.1 0.1 copy.14
  246.2 0.3 fusion.28
  246.5 0.0 copy-start.2
  246.5 0.0 copy-start.3
  246.6 0.4 convolution_multiply_fusion
  247.0 0.1 reshape.119
  247.0 0.5 copy.15
  247.5 1.3 fusion.7
  248.8 0.0 all-gather.14.cloned.1.call-update
  248.9 206.1 %reduce-scatter.5.cloned.1.call-done = bf16[256,128]{0,1:T(8,128)(2,1)} async-done(((bf16[8192,128]{0,1:T(8,128)(2,1)}), bf16[256,128]{0,1:T(8,128)(2,1)}) %reduce-scatter.5.cloned.1.call-update) | async-done | bytes 65552 | tf_op jit(solution)/shard_map/reduce_scatter | solution.py:120
  454.9 224.9 %reduce-scatter.3.cloned.1.call-done = bf16[256,128]{0,1:T(8,128)(2,1)} async-done(((bf16[8192,128]{0,1:T(8,128)(2,1)}), bf16[256,128]{0,1:T(8,128)(2,1)}) %reduce-scatter.3.cloned.1.call-update) | async-done | bytes 65552 | tf_op jit(solution)/shard_map/reduce_scatter | solution.py:93
  679.8 0.0 copy-done.2
  679.8 0.0 copy-done.3
  679.8 0.9 fusion.25
  680.8 5.8 collective-permute-start.1
  686.5 1.3 collective-permute-start
  687.8 1.9 collective-permute-done.1
  689.7 0.0 collective-permute-done
  689.7 66.1 %all-gather.14.cloned.1.call-done = bf16[128,128,256]{2,0,1:T(8,128)(2,1)} async-done(((bf16[8,128,256]{2,0,1:T(8,128)(2,1)}), bf16[128,128,256]{2,0,1:T(8,128)(2,1)}) %all-gather.14.cloned.1.call-update) | async-done | bytes 8388624 | tf_op jit(solution)/shard_map/all_gather | solution.py:142
  755.9 5.7 bitcast_reduce_fusion
  761.6 0.1 copy.19
  761.7 0.9 reshape.146
  762.6 0.6 copy.29
  763.2 0.6 copy.30
  (7 shorter events, 0.1 us)
Async XLA Ops:
  7.2 94.6 %all-gather.10.cloned.1.call-start = ((), (), s32[]{:S(2)}) async-start(), calls=%async_computation.5 | async-start | bytes 4325376 | tf_op jit(solution)/shard_map/all_gather | solution.py:45
  7.9 177.8 %all-gather.12.cloned.1.call-start = ((), (), s32[]{:S(2)}) async-start(), calls=%async_computation.6 | async-start | bytes 2162688 | tf_op jit(solution)/shard_map/all_gather | solution.py:46
  8.6 225.9 %all-gather.8.cloned.1.call-start = ((), (), s32[]{:S(2)}) async-start(), calls=%async_computation.2 | async-start | bytes 2228224 | tf_op jit(solution)/shard_map/all_gather | solution.py:74
  101.8 4.2 copy-start.4
  105.3 0.7 copy-start.1
  106.0 349.0 %reduce-scatter.5.cloned.1.call-start = ((), (), s32[]{:S(2)}) async-start(), calls=%async_computation.4 | async-start | bytes 2162688 | tf_op jit(solution)/shard_map/reduce_scatter | solution.py:120
  241.0 438.8 %reduce-scatter.3.cloned.1.call-start = ((), (), s32[]{:S(2)}) async-start(), calls=%async_computation.3 | async-start | bytes 2162688 | tf_op jit(solution)/shard_map/reduce_scatter | solution.py:93
  246.0 509.8 %all-gather.14.cloned.1.call-start = ((), (), s32[]{:S(2)}) async-start(), calls=%async_computation.7 | async-start | bytes 8912896 | tf_op jit(solution)/shard_map/all_gather | solution.py:142
  246.5 433.3 %copy-start.2 = (bf16[1,2,128,256]{3,2,1,0:T(8,128)(2,1)S(1)}, bf16[1,2,128,256]{3,2,1,0:T(8,128)(2,1)}, u32[]{:S(2)}) copy-start(bf16[1,2,128,256]{3,2,1,0:T(8,128)(2,1)} %param.6) | copy-start | bytes 393220
  246.5 433.3 %copy-start.3 = (bf16[1,128,256]{2,1,0:T(8,128)(2,1)S(1)}, bf16[1,128,256]{2,1,0:T(8,128)(2,1)}, u32[]{:S(2)}) copy-start(bf16[1,128,256]{2,1,0:T(8,128)(2,1)} %param.7) | copy-start | bytes 196612
  680.8 9.0 %collective-permute-start.1 = (bf16[1,128,256]{2,1,0:T(8,128)(2,1)S(1)}, bf16[1,128,256]{2,1,0:T(8,128)(2,1)S(1)}, u32[]{:S(2)}, u32[]{:S(2)}) collective-permute-start(bf16[1,128,256]{2,1,0:T(8,128)(2,1)S(1)} %get-tuple-element.55), channel_id=1, source_target_pairs={{0,480},{32,0},{64,32},{96,64},{128,96},{160,128},{192,160},{224,1... | collective-permute-start | bytes 196616 | tf_op jit(solution)/shard_map/ppermute | solution.py:14
  686.5 3.2 collective-permute-start
Sparse Core Ops, SparseCore 0:
  11.0 90.6 all-gather.9
  104.8 80.7 all-gather.11
  188.4 46.0 all-gather.7
  241.1 213.7 reduce-scatter.4
  459.8 219.9 reduce-scatter.2
  682.3 73.5 all-gather.13
